TPU v7x, 512 devices: a whole 4x8x8 slice. The times are simulated.
512 devices in a mesh: band: 32 (over x, y), seq: 16 (over z, core).
Axes of the slice: x: 4, y: 8, z: 8, core: 2. Of those that a mesh axis runs over, the one named last changes fastest.
Arguments:
- posteriors: bfloat16 [32, 262144], P(None, ('band', 'seq'))
- seed_mask: int32 [262144], P(('band', 'seq')), may hold values 0 or 1
- frame_perm: int32 [512, 512], P(('band', 'seq')), may hold values from 0 to 511, each once within a row
- lengths: int32 [256], replicated, may hold values from 1 to 4096, 262144 in all
- embeddings: bfloat16 [262144, 256], P(('band', 'seq')), may hold values from -12 to 12
- partners: int32 [2048, 32], P(('band', 'seq')), may hold values from 0 to 127, as said below
- levels: int32 [2048, 32], P(('band', 'seq')), may hold values from 1 to 8, as said below
Outputs:
- spread_labels: float32 [32, 262144], P(None, ('band', 'seq'))
Inputs may be any that keep to these rules, and one draw needn't show every extreme that they name: `partners`: within each seq index s, slot k pairs the 128 tiles mutually: if tile number a names b in slot k then b names a in slot k; no tile names itself. `levels`: two tiles paired in slot k carry the same level.
All inputs are finite; a program needn't handle non-finite values. No bound on the sum of `seed_mask` on one device may be relied on, other than what follows from the above.
Results may differ from a plain program's by a relative error of at most 0.007.
Values may be sent and summed in bfloat16 or wider, within the bound.
No kernel may reach another device: no remote copies, remote signals or barrier semaphores. Data moves between devices by JAX's collectives and lax.ppermute only.
A program may use at most 64 MiB of HBM per device.

v0:
```python
import math

import jax
import jax.numpy as jnp
from jax import lax
from jax.sharding import PartitionSpec as P

RADIUS = 64
ITERS = 3


decay_len = 16.0
spread_rate = 0.9


def with_halo(cells, sides, width):
    for axis, dim in sides:
        count = lax.axis_size(axis)
        ends = count - 1
        head = lax.slice_in_dim(cells, 0, width, axis=dim)
        tail = lax.slice_in_dim(cells, cells.shape[dim] - width, cells.shape[dim], axis=dim)
        cells = jnp.concatenate(
            [
                lax.ppermute(tail, axis, [(i, (i + 1) % count) for i in range(ends)]),
                cells,
                lax.ppermute(head, axis, [((i + 1) % count, i) for i in range(ends)]),
            ],
            axis=dim,
        )
    return cells


def on_device(posteriors, seed_mask, frame_perm, lengths, embeddings, partners, levels):
    channels, frames = posteriors.shape
    band_count = lax.axis_size("band")
    groups = lax.axis_size("seq")
    tile_count = frames // 128
    seeded = posteriors * seed_mask.astype(jnp.bfloat16)[None, :]
    ordered = jnp.take(seeded, frame_perm[0], axis=1).reshape(
        channels, band_count, frames // band_count
    )
    arrived = lax.all_to_all(ordered, "band", split_axis=1, concat_axis=1, tiled=True)
    labels = arrived.reshape(channels, frames).astype(jnp.float32)
    device = lax.axis_index("band") * groups + lax.axis_index("seq")
    frame_total = frames * band_count * groups
    window = 128 + 2 * RADIUS
    global_at = device * frames - RADIUS + jnp.arange(frames + 2 * RADIUS, dtype=jnp.int32)
    utt_ends = jnp.cumsum(lengths)
    owner_seg = jnp.sum((utt_ends[None, :] <= global_at[:, None]).astype(jnp.int32), axis=1)
    inside = (global_at >= 0) & (global_at < frame_total)
    tile_off = (jnp.arange(tile_count, dtype=jnp.int32) * 128)[:, None, None]
    win_pos = tile_off + jnp.arange(window, dtype=jnp.int32)[None, :, None]
    row_pos = tile_off + RADIUS + jnp.arange(128, dtype=jnp.int32)[None, None, :]
    offset = jnp.abs(win_pos - row_pos)
    linked = (
        (offset >= 1)
        & (offset <= RADIUS)
        & (owner_seg[win_pos] == owner_seg[row_pos])
        & inside[win_pos]
    )
    band_tiles = jnp.where(
        linked, jnp.exp(-offset.astype(jnp.float32) / decay_len), jnp.float32(0.0)
    ).astype(jnp.bfloat16)
    near_degree = jnp.sum(band_tiles.astype(jnp.float32), axis=1).reshape(frames)
    gathered = lax.all_gather(embeddings, "band", axis=0, tiled=True)
    embed_width = embeddings.shape[1]
    partner_rows = gathered.reshape(-1, 128, embed_width)[partners]
    own_rows = embeddings.reshape(tile_count, 128, embed_width)
    inner_prod = jnp.einsum(
        "tkje,tie->tkji", partner_rows, own_rows, preferred_element_type=jnp.float32
    )
    affinity = (
        jnp.exp(0.5 * (inner_prod / math.sqrt(embed_width)))
        * (levels.astype(jnp.float32) / 8.0)[:, :, None, None]
        / 128.0
    )
    affinity = affinity.astype(jnp.bfloat16)
    far_degree = jnp.sum(affinity.astype(jnp.float32), axis=(1, 2)).reshape(frames)
    norm_scale = 1.0 / jnp.sqrt(near_degree + far_degree)

    def squares(residual):
        return lax.psum(jnp.sum(residual * residual, axis=1), ("band", "seq"))

    solution = jnp.zeros((channels, frames), jnp.float32)
    residual = labels
    direction = labels
    norm_now = squares(residual)
    for iteration in range(ITERS):
        lifted = (norm_scale[None, :] * direction).astype(jnp.bfloat16)
        padded = with_halo(lifted, ((("band", "seq"), 1),), RADIUS)
        windows = jnp.stack(
            [padded[:, position * 128 : position * 128 + window] for position in range(tile_count)],
            axis=0,
        )
        near_term = jnp.einsum(
            "tcw,twa->cta", windows, band_tiles, preferred_element_type=jnp.float32
        ).reshape(channels, frames)
        spread = lax.all_gather(lifted, "band", axis=1, tiled=True).reshape(channels, -1, 128)
        far_tiles = spread[:, partners]
        far_term = jnp.einsum(
            "ctkj,tkji->cti", far_tiles, affinity, preferred_element_type=jnp.float32
        ).reshape(channels, frames)
        image = direction - spread_rate * norm_scale[None, :] * (near_term + far_term)
        curve = lax.psum(jnp.sum(direction * image, axis=1), ("band", "seq"))
        alpha = norm_now / curve
        solution = solution + alpha[:, None] * direction
        residual = residual - alpha[:, None] * image
        norm_next = squares(residual)
        direction = residual + (norm_next / norm_now)[:, None] * direction
        norm_now = norm_next
    return solution


def solution(mesh):
    placed = (
        P(None, ("band", "seq")),
        P(("band", "seq")),
        P(("band", "seq"), None),
        P(),
        P(("band", "seq"), None),
        P(("band", "seq"), None),
        P(("band", "seq"), None),
    )
    return jax.shard_map(
        on_device, mesh=mesh, in_specs=placed, out_specs=P(None, ("band", "seq")), check_vma=False
    )
```

profile of v0, /device:TPU:6, one launch (start us, length us, event | category | flops | bytes accessed | tf_op | source)
XLA Modules:
  0.0 859.8 jit_solution(14141777168958132764)
XLA Ops:
  6.5 0.7 all-gather.5.cloned.1.call-update
  7.9 0.8 broadcast_multiply_fusion
  9.4 1.3 reduce.11
  11.5 1.3 gather_fusion
  13.0 0.8 reshape.489
  13.7 10.2 %all-to-all-start = ((bf16[32,2,256]{2,1,0:T(2,128)(2,1)}), bf16[32,2,256]{2,1,0:T(2,128)(2,1)S(1)}, u32[]{:S(2)}, u32[]{:S(2)}) async-start(bf16[32,2,256]{2,1,0:T(2,128)(2,1)} %reshape.489), calls=%async_computation | async-start | bytes 65536 | tf_op jit(solution)/shard_map/all_to_all | solution.py:42
  24.0 1.0 reduce-window.9
  25.7 4.5 gather_fusion.1
  30.3 2.3 gather_fusion.2
  32.6 6.8 gather_fusion.3
  40.6 76.0 %all-gather.5.cloned.1.call-done = bf16[16384,256]{1,0:T(8,128)(2,1)} async-done(((bf16[512,256]{1,0:T(8,128)(2,1)}), bf16[16384,256]{1,0:T(8,128)(2,1)}) %all-gather.5.cloned.1.call-update) | async-done | bytes 8388624 | tf_op jit(solution)/shard_map/all_gather | solution.py:65
  116.6 10.0 %gather_fusion.4 = bf16[128,128,256]{2,1,0:T(8,128)(2,1)} fusion(bf16[128,128,256]{2,1,0:T(8,128)(2,1)} %bitcast.161, s32[1024]{0:T(1024)S(1)} %pad_clamp_fusion), kind=kCustom, calls=%fused_computation.4 | custom fusion | bytes 16777728 | tf_op jit(solution)/shard_map/gather | solution.py:67
  126.6 7.7 convert_reduce_fusion
  135.0 0.8 fusion.72
  135.8 1.9 collective-permute-start
  137.7 7.9 collective-permute-start.1
  145.7 1.2 collective-permute-done.1
  146.9 0.9 fusion.49
  148.5 62.3 %all-gather.7.cloned.1.call-done = bf16[32,16384]{1,0:T(8,128)(2,1)} async-done(((bf16[32,512]{1,0:T(8,128)(2,1)}), bf16[32,16384]{1,0:T(8,128)(2,1)}) %all-gather.7.cloned.1.call-update) | async-done | bytes 1048592 | tf_op jit(solution)/shard_map/all_gather | solution.py:98
  210.7 1.4 copy_bitcast_fusion.2
  212.1 0.8 gather_fusion.5
  212.9 2.9 fusion.3
  216.2 95.8 %all-reduce = (f32[32]{0:T(128)S(1)}, f32[32]{0:T(128)S(1)}) all-reduce(f32[32]{0:T(128)S(1)} %get-tuple-element.6, f32[32]{0:T(128)S(1)} %get-tuple-element.5), channel_id=1, replica_groups=mesh['band'=32,'seq'=16] {'band','seq'}, use_global_device_ids=true, to_apply=%region_1.2 | all-reduce | flops 64 | bytes 512 | tf_op jit(solution)/shard_map/psum | solution.py:82
  312.2 95.8 %psum.44 = f32[32]{0:T(128)S(1)} all-reduce(f32[32]{0:T(128)S(1)} %multiply_reduce_fusion.2), channel_id=1, replica_groups=mesh['band'=32,'seq'=16] {'band','seq'}, use_global_device_ids=true, to_apply=%region_10.11 | all-reduce | flops 32 | bytes 256 | tf_op jit(solution)/shard_map/psum | solution.py:82
  408.0 0.7 multiply_convert_fusion.2
  408.8 0.8 fusion.71
  409.6 1.9 collective-permute-start.2
  411.5 8.0 collective-permute-start.3
  419.5 1.2 collective-permute-done.3
  420.7 0.9 fusion.47
  422.2 58.7 %all-gather.9.cloned.1.call-done = bf16[32,16384]{1,0:T(8,128)(2,1)} async-done(((bf16[32,512]{1,0:T(8,128)(2,1)}), bf16[32,16384]{1,0:T(8,128)(2,1)}) %all-gather.9.cloned.1.call-update) | async-done | bytes 1048592 | tf_op jit(solution)/shard_map/all_gather | solution.py:98
  480.9 1.4 copy_bitcast_fusion.1
  482.3 0.8 gather_fusion.6
  483.1 2.9 fusion.2
  486.4 95.8 %psum.45 = f32[32]{0:T(128)S(1)} all-reduce(f32[32]{0:T(128)S(1)} %multiply_reduce_fusion.1), channel_id=1, replica_groups=mesh['band'=32,'seq'=16] {'band','seq'}, use_global_device_ids=true, to_apply=%region_12.13 | all-reduce | flops 32 | bytes 256 | tf_op jit(solution)/shard_map/psum | solution.py:104
  582.4 95.8 %psum.46 = f32[32]{0:T(128)S(1)} all-reduce(f32[32]{0:T(128)S(1)} %multiply_reduce_fusion), channel_id=1, replica_groups=mesh['band'=32,'seq'=16] {'band','seq'}, use_global_device_ids=true, to_apply=%region_14.15 | all-reduce | flops 32 | bytes 256 | tf_op jit(solution)/shard_map/psum | solution.py:82
  678.3 0.7 multiply_convert_fusion.1
  679.0 0.8 fusion.70
  679.8 1.9 collective-permute-start.4
  681.7 7.9 collective-permute-start.5
  689.6 1.3 collective-permute-done.5
  690.9 0.9 fusion.45
  692.5 58.8 %all-gather.11.cloned.1.call-done = bf16[32,16384]{1,0:T(8,128)(2,1)} async-done(((bf16[32,512]{1,0:T(8,128)(2,1)}), bf16[32,16384]{1,0:T(8,128)(2,1)}) %all-gather.11.cloned.1.call-update) | async-done | bytes 1048592 | tf_op jit(solution)/shard_map/all_gather | solution.py:98
  751.2 1.4 copy_bitcast_fusion
  752.6 0.8 gather_fusion.7
  753.4 2.9 fusion.1
  756.7 95.8 %psum.47 = f32[32]{0:T(128)S(1)} all-reduce(f32[32]{0:T(128)S(1)} %fusion.12), channel_id=1, replica_groups=mesh['band'=32,'seq'=16] {'band','seq'}, use_global_device_ids=true, to_apply=%region_16.17 | all-reduce | flops 32 | bytes 256 | tf_op jit(solution)/shard_map/psum | solution.py:104
  852.6 0.7 multiply_add_fusion
  (70 shorter events, 8.1 us)
Async XLA Ops:
  6.5 32.9 %copy-start.1 = (s32[4,32]{1,0:T(4,128)S(1)}, s32[4,32]{1,0:T(4,128)}, u32[]{:S(2)}) copy-start(s32[4,32]{1,0:T(4,128)} %param.12) | copy-start | bytes 1540
  6.5 33.8 %copy-start.2 = (s32[4,32]{1,0:T(4,128)S(1)}, s32[4,32]{1,0:T(4,128)}, u32[]{:S(2)}) copy-start(s32[4,32]{1,0:T(4,128)} %param.13) | copy-start | bytes 1540
  6.5 110.0 %all-gather.5.cloned.1.call-start = ((), (), s32[]{:S(2)}) async-start(), calls=%async_computation.1 | async-start | bytes 8650752 | tf_op jit(solution)/shard_map/all_gather | solution.py:65
  13.7 26.6 %all-to-all-start = ((bf16[32,2,256]{2,1,0:T(2,128)(2,1)}), bf16[32,2,256]{2,1,0:T(2,128)(2,1)S(1)}, u32[]{:S(2)}, u32[]{:S(2)}) async-start(bf16[32,2,256]{2,1,0:T(2,128)(2,1)} %reshape.489), calls=%async_computation | async-start | bytes 65536 | tf_op jit(solution)/shard_map/all_to_all | solution.py:42
  24.0 186.7 %all-gather.7.cloned.1.call-start = ((), (), s32[]{:S(2)}) async-start(), calls=%async_computation.2 | async-start | bytes 1081344 | tf_op jit(solution)/shard_map/all_gather | solution.py:98
  116.6 10.0 %copy-start = (bf16[512,256]{1,0:T(8,128)(2,1)S(1)}, bf16[512,256]{1,0:T(8,128)(2,1)}, u32[]{:S(2)}) copy-start(bf16[512,256]{1,0:T(8,128)(2,1)} %param.11) | copy-start | bytes 786436
  135.0 346.0 %all-gather.9.cloned.1.call-start = ((), (), s32[]{:S(2)}) async-start(), calls=%async_computation.3 | async-start | bytes 1081344 | tf_op jit(solution)/shard_map/all_gather | solution.py:98
  135.8 9.9 %collective-permute-start = (bf16[32,64]{1,0:T(8,128)(2,1)S(1)}, bf16[32,64]{1,0:T(8,128)(2,1)S(1)}, u32[]{:S(2)}, u32[]{:S(2)}) collective-permute-start(bf16[32,64]{1,0:T(8,128)(2,1)S(1)} %get-tuple-element.29), channel_id=1, source_target_pairs={{0,1},{1,2},{2,3},{3,4},{4,5},{5,6},{6,7},{7,8},{8,9},{9,10},{10,1... | collective-permute-start | bytes 12296 | tf_op jit(solution)/shard_map/ppermute | solution.py:24
  137.7 9.2 %collective-permute-start.1 = (bf16[32,64]{1,0:T(8,128)(2,1)S(1)}, bf16[32,64]{1,0:T(8,128)(2,1)S(1)}, u32[]{:S(2)}, u32[]{:S(2)}) collective-permute-start(bf16[32,64]{1,0:T(8,128)(2,1)S(1)} %get-tuple-element.30), channel_id=1, source_target_pairs={{1,0},{2,1},{3,2},{4,3},{5,4},{6,5},{7,6},{8,7},{9,8},{10,9},{11,1... | collective-permute-start | bytes 12296 | tf_op jit(solution)/shard_map/ppermute | solution.py:26
  408.7 342.5 %all-gather.11.cloned.1.call-start = ((), (), s32[]{:S(2)}) async-start(), calls=%async_computation.4 | async-start | bytes 1081344 | tf_op jit(solution)/shard_map/all_gather | solution.py:98
  409.6 10.0 %collective-permute-start.2 = (bf16[32,64]{1,0:T(8,128)(2,1)S(1)}, bf16[32,64]{1,0:T(8,128)(2,1)S(1)}, u32[]{:S(2)}, u32[]{:S(2)}) collective-permute-start(bf16[32,64]{1,0:T(8,128)(2,1)S(1)} %get-tuple-element.23), channel_id=1, source_target_pairs={{0,1},{1,2},{2,3},{3,4},{4,5},{5,6},{6,7},{7,8},{8,9},{9,10},{10,1... | collective-permute-start | bytes 12296 | tf_op jit(solution)/shard_map/ppermute | solution.py:24
  411.5 9.2 %collective-permute-start.3 = (bf16[32,64]{1,0:T(8,128)(2,1)S(1)}, bf16[32,64]{1,0:T(8,128)(2,1)S(1)}, u32[]{:S(2)}, u32[]{:S(2)}) collective-permute-start(bf16[32,64]{1,0:T(8,128)(2,1)S(1)} %get-tuple-element.24), channel_id=1, source_target_pairs={{1,0},{2,1},{3,2},{4,3},{5,4},{6,5},{7,6},{8,7},{9,8},{10,9},{11,1... | collective-permute-start | bytes 12296 | tf_op jit(solution)/shard_map/ppermute | solution.py:26
  679.8 9.8 %collective-permute-start.4 = (bf16[32,64]{1,0:T(8,128)(2,1)S(1)}, bf16[32,64]{1,0:T(8,128)(2,1)S(1)}, u32[]{:S(2)}, u32[]{:S(2)}) collective-permute-start(bf16[32,64]{1,0:T(8,128)(2,1)S(1)} %get-tuple-element.17), channel_id=1, source_target_pairs={{0,1},{1,2},{2,3},{3,4},{4,5},{5,6},{6,7},{7,8},{8,9},{9,10},{10,1... | collective-permute-start | bytes 12296 | tf_op jit(solution)/shard_map/ppermute | solution.py:24
  681.7 9.2 %collective-permute-start.5 = (bf16[32,64]{1,0:T(8,128)(2,1)S(1)}, bf16[32,64]{1,0:T(8,128)(2,1)S(1)}, u32[]{:S(2)}, u32[]{:S(2)}) collective-permute-start(bf16[32,64]{1,0:T(8,128)(2,1)S(1)} %get-tuple-element.18), channel_id=1, source_target_pairs={{1,0},{2,1},{3,2},{4,3},{5,4},{6,5},{7,6},{8,7},{9,8},{10,9},{11,1... | collective-permute-start | bytes 12296 | tf_op jit(solution)/shard_map/ppermute | solution.py:26
Sparse Core Ops, SparseCore 0:
  10.5 105.9 all-gather.4
  135.1 75.6 all-gather.6
  408.8 72.0 all-gather.8
  679.1 72.0 all-gather.10
where the time goes:
time: 864 us; the launch traced here: 860 us
  blocking collectives  479 us (55%)
  waiting for transfers between devices  260 us (30%)
  starting transfers between devices  39.9 us (5%)
  local copies, waits for them, and re-layouts  36.3 us (4%)
  matrix products  18.3 us (2%)
  between operations  13.5 us (2%)
  other arithmetic  12.5 us (1%)
    psum x3, blocking collectives, squares(): return lax.psum(jnp.sum(residual * residual, axis=1), ('band', 'seq'))  287 us
    psum x2, blocking collectives, on_device(): curve = lax.psum(jnp.sum(direction * image, axis=1), ('band', 'seq'))  192 us
    all_gather x3, waiting for transfers between devices, on_device(): lax.all_gather(lifted, 'band', axis=1, tiled=True)  180 us
    all_gather x1, waiting for transfers between devices, on_device(): gathered = lax.all_gather(embeddings, 'band', axis=0, tiled=True)  76 us
    ppermute x3, starting transfers between devices, with_halo(): lax.ppermute(head, axis, [((i + 1) % count, i) for i in range(ends)])  23.8 us
  transfers between devices with their start and end apart: 11, of which 7 were waited for; matrix products, arithmetic and copies ran while one was open for 3% of the time, Pallas kernels for 0%

commit v1 on v0

--- a/solution.py
+++ b/solution.py
@@ -28,6 +28,40 @@
             axis=dim,
         )
     return cells
+
+
+def butterfly_sum(values):
+    count = lax.axis_size("band") * lax.axis_size("seq")
+    for bit in range(count.bit_length() - 1):
+        step = 1 << bit
+        values = values + lax.ppermute(
+            values, ("band", "seq"), [(i, i ^ step) for i in range(count)]
+        )
+    return values
+
+
+def band_exchange(block):
+    count = lax.axis_size("band")
+    bits = count.bit_length() - 1
+    me = lax.axis_index("band")
+    held = block[None]
+    for bit in reversed(range(bits)):
+        step = 1 << bit
+        other = lax.ppermute(held, "band", [(i, i ^ step) for i in range(count)])
+        low = ((me >> bit) & 1) == 0
+        held = jnp.where(
+            low,
+            jnp.concatenate([held, other], axis=0),
+            jnp.concatenate([other, held], axis=0),
+        )
+    return held
+
+
+def bit_reverse(values, bits):
+    out = jnp.zeros_like(values)
+    for bit in range(bits):
+        out = out | (((values >> bit) & 1) << (bits - 1 - bit))
+    return out
 
 
 def on_device(posteriors, seed_mask, frame_perm, lengths, embeddings, partners, levels):
@@ -78,8 +112,12 @@
     far_degree = jnp.sum(affinity.astype(jnp.float32), axis=(1, 2)).reshape(frames)
     norm_scale = 1.0 / jnp.sqrt(near_degree + far_degree)
 
+    per_band = frames // 128
+    band_bits = band_count.bit_length() - 1
+    held_partners = bit_reverse(partners // per_band, band_bits) * per_band + partners % per_band
+
     def squares(residual):
-        return lax.psum(jnp.sum(residual * residual, axis=1), ("band", "seq"))
+        return butterfly_sum(jnp.sum(residual * residual, axis=1))
 
     solution = jnp.zeros((channels, frames), jnp.float32)
     residual = labels
@@ -95,13 +133,14 @@
         near_term = jnp.einsum(
             "tcw,twa->cta", windows, band_tiles, preferred_element_type=jnp.float32
         ).reshape(channels, frames)
-        spread = lax.all_gather(lifted, "band", axis=1, tiled=True).reshape(channels, -1, 128)
-        far_tiles = spread[:, partners]
+        held = band_exchange(lifted).reshape(band_count, channels, -1, 128)
+        spread = jnp.transpose(held, (1, 0, 2, 3)).reshape(channels, -1, 128)
+        far_tiles = spread[:, held_partners]
         far_term = jnp.einsum(
             "ctkj,tkji->cti", far_tiles, affinity, preferred_element_type=jnp.float32
         ).reshape(channels, frames)
         image = direction - spread_rate * norm_scale[None, :] * (near_term + far_term)
-        curve = lax.psum(jnp.sum(direction * image, axis=1), ("band", "seq"))
+        curve = butterfly_sum(jnp.sum(direction * image, axis=1))
         alpha = norm_now / curve
         solution = solution + alpha[:, None] * direction
         residual = residual - alpha[:, None] * image

time: 864 us -> 626 us (0.72)
  blocking collectives: 479 us -> 0 us
  starting transfers between devices: 39.9 us -> 256 us
  waiting for transfers between devices: 260 us -> 288 us
    psum x5 -> x0, blocking collectives: 479 us -> none  [the longest x3 287 us: squares(): return lax.psum(jnp.sum(residual * residual, axis=1), ('band', 'seq'))]
    ppermute x0 -> x69, starting transfers between devices: none -> 219 us  [the longest x54 170 us: butterfly_sum(): lax.ppermute(values, ('band', 'seq'), [(i, i ^ step) for i in range(count)])]
    ppermute x0 -> x69, waiting for transfers between devices: none -> 205 us  [the longest x54 131 us: butterfly_sum(): lax.ppermute(values, ('band', 'seq'), [(i, i ^ step) for i in range(count)])]
    all_gather x3 -> x0, waiting for transfers between devices: 180 us -> none  [on_device(): lax.all_gather(lifted, 'band', axis=1, tiled=True)]
  transfers between devices with their start and end apart: 11 -> 77, of which waited for: 7 -> 55; matrix products, arithmetic and copies ran while one was open for 3% -> 5% of each run, Pallas kernels for 0% -> 0%
where the time goes in v1:
time: 626 us; the launch traced here: 624 us
  waiting for transfers between devices  288 us (46%)
  starting transfers between devices  256 us (41%)
  local copies, waits for them, and re-layouts  31.8 us (5%)
  matrix products  18.4 us (3%)
  other arithmetic  15.4 us (2%)
  between operations  14.9 us (2%)
    ppermute x54, starting transfers between devices, butterfly_sum(): lax.ppermute(values, ('band', 'seq'), [(i, i ^ step) for i in range(count)])  170 us
    ppermute x54, waiting for transfers between devices, butterfly_sum(): lax.ppermute(values, ('band', 'seq'), [(i, i ^ step) for i in range(count)])  131 us
    all_gather x1, waiting for transfers between devices, on_device(): gathered = lax.all_gather(embeddings, 'band', axis=0, tiled=True)  76.1 us
    ppermute x15, waiting for transfers between devices, band_exchange(): other = lax.ppermute(held, 'band', [(i, i ^ step) for i in range(count)])  73.8 us
    ppermute x15, starting transfers between devices, band_exchange(): other = lax.ppermute(held, 'band', [(i, i ^ step) for i in range(count)])  48.7 us
    ppermute x3, starting transfers between devices, with_halo(): lax.ppermute(head, axis, [((i + 1) % count, i) for i in range(ends)])  20.7 us
  transfers between devices with their start and end apart: 77, of which 55 were waited for; matrix products, arithmetic and copies ran while one was open for 5% of the time, Pallas kernels for 0%

profile of v1, /device:TPU:6, one launch (start us, length us, event | category | flops | bytes accessed | tf_op | source)
XLA Modules:
  0.0 624.0 jit_solution(12297061556990700198)
XLA Ops:
  13.7 10.2 %all-to-all-start = ((bf16[32,2,256]{2,1,0:T(2,128)(2,1)}), bf16[32,2,256]{2,1,0:T(2,128)(2,1)S(1)}, u32[]{:S(2)}, u32[]{:S(2)}) async-start(bf16[32,2,256]{2,1,0:T(2,128)(2,1)} %reshape.881), calls=%async_computation | async-start | bytes 65536 | tf_op jit(solution)/shard_map/all_to_all | solution.py:76
  25.6 4.5 gather_fusion.1
  32.6 6.8 %gather_fusion.3 = pred[1024]{0:T(1024)(128)(4,1)S(1)} fusion(pred[640]{0:T(1024)(128)(4,1)S(1)} %compare_and_fusion.1, s32[1024]{0:T(1024)S(1)} %broadcast_clamp_fusion), kind=kCustom, calls=%fused_computation.3 | custom fusion | bytes 6144 | tf_op jit(solution)/shard_map/gather | solution.py:93
  40.6 76.1 %all-gather.2.cloned.1.call-done = bf16[16384,256]{1,0:T(8,128)(2,1)} async-done(((bf16[512,256]{1,0:T(8,128)(2,1)}), bf16[16384,256]{1,0:T(8,128)(2,1)}) %all-gather.2.cloned.1.call-update) | async-done | bytes 8388624 | tf_op jit(solution)/shard_map/all_gather | solution.py:99
  116.7 10.1 %gather_fusion.4 = bf16[128,128,256]{2,1,0:T(8,128)(2,1)} fusion(bf16[128,128,256]{2,1,0:T(8,128)(2,1)} %bitcast.156, s32[1024]{0:T(1024)S(1)} %pad_clamp_fusion.1), kind=kCustom, calls=%fused_computation.4 | custom fusion | bytes 16777728 | tf_op jit(solution)/shard_map/gather | solution.py:101
  126.8 7.8 %convert_reduce_fusion = (f32[4,128]{1,0:T(4,128)S(1)}, bf16[4,32,128,128]{3,2,1,0:T(8,128)(2,1)}) fusion(f32[4,32]{1,0:T(4,128)S(1)} %convert_multiply_fusion.3, bf16[4,32,128,256]{3,2,1,0:T(8,128)(2,1)} %bitcast.157, bf16[4,128,256,1]{2,1,3,0:T(8,128)(2,1)S(1)} %bitcast.174), kind=kOutput, calls=%fused_computation.8 | convolution fusion | flops 1086324224 | bytes 12847616 | tf_op jit(solution)/shard_map/tkje,tie->tkji/dot_general | solution.py:103
  134.6 4.0 collective-permute-start.11
  148.1 5.1 collective-permute-start.13
  153.3 5.0 collective-permute-start.10
  167.6 8.0 %collective-permute-done.14 = bf16[8,32,512]{2,1,0:T(8,128)(2,1)S(1)} collective-permute-done((bf16[8,32,512]{2,1,0:T(8,128)(2,1)S(1)}, bf16[8,32,512]{2,1,0:T(8,128)(2,1)S(1)}, u32[]{:S(2)}, u32[]{:S(2)}) %collective-permute-start.14) | collective-permute-done | bytes 262176 | tf_op jit(solution)/shard_map/ppermute | solution.py:50
  179.6 10.9 %collective-permute-done.15 = bf16[16,32,512]{2,1,0:T(8,128)(2,1)S(1)} collective-permute-done((bf16[16,32,512]{2,1,0:T(8,128)(2,1)S(1)}, bf16[16,32,512]{2,1,0:T(8,128)(2,1)S(1)}, u32[]{:S(2)}, u32[]{:S(2)}) %collective-permute-start.15) | collective-permute-done | bytes 524320 | tf_op jit(solution)/shard_map/ppermute | solution.py:50
  206.3 6.4 %collective-permute-start.2 = (f32[32]{0:T(128)S(1)}, f32[32]{0:T(128)S(1)}, u32[]{:S(2)}, u32[]{:S(2)}) collective-permute-start(f32[32]{0:T(128)S(1)} %add.470), channel_id=1, source_target_pairs={{0,4},{1,5},{2,6},{3,7},{4,0},{5,1},{6,2},{7,3},{8,12},{9,13},{10,... | collective-permute-start | bytes 392 | tf_op jit(solution)/shard_map/ppermute | solution.py:37
  216.2 4.0 collective-permute-start.3
  220.2 5.7 collective-permute-start.19
  238.7 5.3 collective-permute-start.6
  244.0 4.4 collective-permute-start.22
  256.5 4.6 collective-permute-start.8
  263.9 4.2 collective-permute-done.24
  283.0 4.8 collective-permute-start.28
  287.8 4.5 collective-permute-done.28
  297.7 4.8 collective-permute-start.30
  304.1 4.4 collective-permute-start.31
  308.5 4.9 collective-permute-done.31
  321.7 4.1 collective-permute-done.33
  328.6 4.6 collective-permute-done.36
  335.1 4.2 collective-permute-done.37
  339.4 4.4 collective-permute-start.38
  343.9 7.2 %collective-permute-done.38 = bf16[4,32,512]{2,1,0:T(8,128)(2,1)S(1)} collective-permute-done((bf16[4,32,512]{2,1,0:T(8,128)(2,1)S(1)}, bf16[4,32,512]{2,1,0:T(8,128)(2,1)S(1)}, u32[]{:S(2)}, u32[]{:S(2)}) %collective-permute-start.38) | collective-permute-done | bytes 131104 | tf_op jit(solution)/shard_map/ppermute | solution.py:50
  351.1 5.2 collective-permute-start.39
  358.3 7.9 %collective-permute-start.35 = (bf16[32,64]{1,0:T(8,128)(2,1)S(1)}, bf16[32,64]{1,0:T(8,128)(2,1)S(1)}, u32[]{:S(2)}, u32[]{:S(2)}) collective-permute-start(bf16[32,64]{1,0:T(8,128)(2,1)S(1)} %get-tuple-element.28), channel_id=1, source_target_pairs={{1,0},{2,1},{3,2},{4,3},{5,4},{6,5},{7,6},{8,7},{9,8},{10,9},{11,1... | collective-permute-start | bytes 12296 | tf_op jit(solution)/shard_map/ppermute | solution.py:26
  371.5 8.9 %collective-permute-done.40 = bf16[16,32,512]{2,1,0:T(8,128)(2,1)S(1)} collective-permute-done((bf16[16,32,512]{2,1,0:T(8,128)(2,1)S(1)}, bf16[16,32,512]{2,1,0:T(8,128)(2,1)S(1)}, u32[]{:S(2)}, u32[]{:S(2)}) %collective-permute-start.40) | collective-permute-done | bytes 524320 | tf_op jit(solution)/shard_map/ppermute | solution.py:50
  404.6 5.4 collective-permute-done.44
  417.8 4.0 collective-permute-done.46
  424.2 6.9 %collective-permute-done.47 = f32[32]{0:T(128)S(1)} collective-permute-done((f32[32]{0:T(128)S(1)}, f32[32]{0:T(128)S(1)}, u32[]{:S(2)}, u32[]{:S(2)}) %collective-permute-start.47) | collective-permute-done | bytes 160 | tf_op jit(solution)/shard_map/ppermute | solution.py:37
  462.4 5.4 collective-permute-done.53
  475.5 4.0 collective-permute-done.55
  482.0 6.9 %collective-permute-done.56 = f32[32]{0:T(128)S(1)} collective-permute-done((f32[32]{0:T(128)S(1)}, f32[32]{0:T(128)S(1)}, u32[]{:S(2)}, u32[]{:S(2)}) %collective-permute-start.56) | collective-permute-done | bytes 160 | tf_op jit(solution)/shard_map/ppermute | solution.py:37
  497.3 3.9 collective-permute-done.58
  504.2 4.4 collective-permute-done.61
  517.4 8.6 %collective-permute-done.63 = bf16[4,32,512]{2,1,0:T(8,128)(2,1)S(1)} collective-permute-done((bf16[4,32,512]{2,1,0:T(8,128)(2,1)S(1)}, bf16[4,32,512]{2,1,0:T(8,128)(2,1)S(1)}, u32[]{:S(2)}, u32[]{:S(2)}) %collective-permute-start.63) | collective-permute-done | bytes 131104 | tf_op jit(solution)/shard_map/ppermute | solution.py:50
  526.0 4.8 collective-permute-start.64
  532.8 7.9 %collective-permute-start.60 = (bf16[32,64]{1,0:T(8,128)(2,1)S(1)}, bf16[32,64]{1,0:T(8,128)(2,1)S(1)}, u32[]{:S(2)}, u32[]{:S(2)}) collective-permute-start(bf16[32,64]{1,0:T(8,128)(2,1)S(1)} %get-tuple-element.22), channel_id=1, source_target_pairs={{1,0},{2,1},{3,2},{4,3},{5,4},{6,5},{7,6},{8,7},{9,8},{10,9},{11,1... | collective-permute-start | bytes 12296 | tf_op jit(solution)/shard_map/ppermute | solution.py:26
  545.9 7.3 %collective-permute-done.65 = bf16[16,32,512]{2,1,0:T(8,128)(2,1)S(1)} collective-permute-done((bf16[16,32,512]{2,1,0:T(8,128)(2,1)S(1)}, bf16[16,32,512]{2,1,0:T(8,128)(2,1)S(1)}, u32[]{:S(2)}, u32[]{:S(2)}) %collective-permute-start.65) | collective-permute-done | bytes 524320 | tf_op jit(solution)/shard_map/ppermute | solution.py:50
  573.6 4.5 collective-permute-start.69
  578.2 4.8 collective-permute-done.69
  594.7 4.2 collective-permute-start.72
  598.9 5.1 collective-permute-done.72
  612.3 4.1 collective-permute-done.74
  (292 shorter events, 263.8 us)
Async XLA Ops:
  6.5 110.2 %all-gather.2.cloned.1.call-start = ((), (), s32[]{:S(2)}) async-start(), calls=%async_computation.1 | async-start | bytes 8650752 | tf_op jit(solution)/shard_map/all_gather | solution.py:99
  13.7 26.6 %all-to-all-start = ((bf16[32,2,256]{2,1,0:T(2,128)(2,1)}), bf16[32,2,256]{2,1,0:T(2,128)(2,1)S(1)}, u32[]{:S(2)}, u32[]{:S(2)}) async-start(bf16[32,2,256]{2,1,0:T(2,128)(2,1)} %reshape.881), calls=%async_computation | async-start | bytes 65536 | tf_op jit(solution)/shard_map/all_to_all | solution.py:76
  134.6 7.3 %collective-permute-start.11 = (bf16[1,32,512]{2,1,0:T(8,128)(2,1)S(1)}, bf16[1,32,512]{2,1,0:T(8,128)(2,1)S(1)}, u32[]{:S(2)}, u32[]{:S(2)}) collective-permute-start(bf16[1,32,512]{2,1,0:T(8,128)(2,1)S(1)} %multiply_convert_fusion.5), channel_id=1, source_target_pairs={{0,256},{16,272},{32,288},{48,304},{64,320},{80,336},{96,352},{112... | collective-permute-start | bytes 98312 | tf_op jit(solution)/shard_map/ppermute | solution.py:50
  148.1 12.1 %collective-permute-start.13 = (bf16[4,32,512]{2,1,0:T(8,128)(2,1)S(1)}, bf16[4,32,512]{2,1,0:T(8,128)(2,1)S(1)}, u32[]{:S(2)}, u32[]{:S(2)}) collective-permute-start(bf16[4,32,512]{2,1,0:T(8,128)(2,1)S(1)} %maximum_select_fusion.16), channel_id=1, source_target_pairs={{0,64},{16,80},{32,96},{48,112},{64,0},{80,16},{96,32},{112,48},{1... | collective-permute-start | bytes 393224 | tf_op jit(solution)/shard_map/ppermute | solution.py:50
  153.3 10.6 %collective-permute-start.10 = (bf16[32,64]{1,0:T(8,128)(2,1)S(1)}, bf16[32,64]{1,0:T(8,128)(2,1)S(1)}, u32[]{:S(2)}, u32[]{:S(2)}) collective-permute-start(bf16[32,64]{1,0:T(8,128)(2,1)S(1)} %get-tuple-element.34), channel_id=1, source_target_pairs={{1,0},{2,1},{3,2},{4,3},{5,4},{6,5},{7,6},{8,7},{9,8},{10,9},{11,1... | collective-permute-start | bytes 12296 | tf_op jit(solution)/shard_map/ppermute | solution.py:26
  158.3 9.2 %collective-permute-start.9 = (bf16[32,64]{1,0:T(8,128)(2,1)S(1)}, bf16[32,64]{1,0:T(8,128)(2,1)S(1)}, u32[]{:S(2)}, u32[]{:S(2)}) collective-permute-start(bf16[32,64]{1,0:T(8,128)(2,1)S(1)} %get-tuple-element.33), channel_id=1, source_target_pairs={{0,1},{1,2},{2,3},{3,4},{4,5},{5,6},{6,7},{7,8},{8,9},{9,10},{10,1... | collective-permute-start | bytes 12296 | tf_op jit(solution)/shard_map/ppermute | solution.py:24
  160.3 15.3 %collective-permute-start.14 = (bf16[8,32,512]{2,1,0:T(8,128)(2,1)S(1)}, bf16[8,32,512]{2,1,0:T(8,128)(2,1)S(1)}, u32[]{:S(2)}, u32[]{:S(2)}) collective-permute-start(bf16[8,32,512]{2,1,0:T(8,128)(2,1)S(1)} %maximum_select_fusion.10), channel_id=1, source_target_pairs={{0,32},{16,48},{32,0},{48,16},{64,96},{80,112},{96,64},{112,80},{1... | collective-permute-start | bytes 786440 | tf_op jit(solution)/shard_map/ppermute | solution.py:50
  175.7 14.8 %collective-permute-start.15 = (bf16[16,32,512]{2,1,0:T(8,128)(2,1)S(1)}, bf16[16,32,512]{2,1,0:T(8,128)(2,1)S(1)}, u32[]{:S(2)}, u32[]{:S(2)}) collective-permute-start(bf16[16,32,512]{2,1,0:T(8,128)(2,1)S(1)} %maximum_select_fusion.4), channel_id=1, source_target_pairs={{0,16},{16,0},{32,48},{48,32},{64,80},{80,64},{96,112},{112,96},{1... | collective-permute-start | bytes 1572872 | tf_op jit(solution)/shard_map/ppermute | solution.py:50
  204.0 8.7 %collective-permute-start.17 = (f32[32]{0:T(128)S(1)}, f32[32]{0:T(128)S(1)}, u32[]{:S(2)}, u32[]{:S(2)}) collective-permute-start(f32[32]{0:T(128)S(1)} %add.505), channel_id=1, source_target_pairs={{0,2},{1,3},{2,0},{3,1},{4,6},{5,7},{6,4},{7,5},{8,10},{9,11},{10,... | collective-permute-start | bytes 392 | tf_op jit(solution)/shard_map/ppermute | solution.py:37
  206.3 9.9 %collective-permute-start.2 = (f32[32]{0:T(128)S(1)}, f32[32]{0:T(128)S(1)}, u32[]{:S(2)}, u32[]{:S(2)}) collective-permute-start(f32[32]{0:T(128)S(1)} %add.470), channel_id=1, source_target_pairs={{0,4},{1,5},{2,6},{3,7},{4,0},{5,1},{6,2},{7,3},{8,12},{9,13},{10,... | collective-permute-start | bytes 392 | tf_op jit(solution)/shard_map/ppermute | solution.py:37
  212.7 7.5 %collective-permute-start.18 = (f32[32]{0:T(128)S(1)}, f32[32]{0:T(128)S(1)}, u32[]{:S(2)}, u32[]{:S(2)}) collective-permute-start(f32[32]{0:T(128)S(1)} %add.506), channel_id=1, source_target_pairs={{0,4},{1,5},{2,6},{3,7},{4,0},{5,1},{6,2},{7,3},{8,12},{9,13},{10,... | collective-permute-start | bytes 392 | tf_op jit(solution)/shard_map/ppermute | solution.py:37
  216.2 9.8 %collective-permute-start.3 = (f32[32]{0:T(128)S(1)}, f32[32]{0:T(128)S(1)}, u32[]{:S(2)}, u32[]{:S(2)}) collective-permute-start(f32[32]{0:T(128)S(1)} %add.471), channel_id=1, source_target_pairs={{0,8},{1,9},{2,10},{3,11},{4,12},{5,13},{6,14},{7,15},{8,0},{9,1},... | collective-permute-start | bytes 392 | tf_op jit(solution)/shard_map/ppermute | solution.py:37
  220.2 9.3 %collective-permute-start.19 = (f32[32]{0:T(128)S(1)}, f32[32]{0:T(128)S(1)}, u32[]{:S(2)}, u32[]{:S(2)}) collective-permute-start(f32[32]{0:T(128)S(1)} %add.507), channel_id=1, source_target_pairs={{0,8},{1,9},{2,10},{3,11},{4,12},{5,13},{6,14},{7,15},{8,0},{9,1},... | collective-permute-start | bytes 392 | tf_op jit(solution)/shard_map/ppermute | solution.py:37
  231.9 6.8 %collective-permute-start.5 = (f32[32]{0:T(128)S(1)}, f32[32]{0:T(128)S(1)}, u32[]{:S(2)}, u32[]{:S(2)}) collective-permute-start(f32[32]{0:T(128)S(1)} %add.473), channel_id=1, source_target_pairs={{0,32},{1,33},{2,34},{3,35},{4,36},{5,37},{6,38},{7,39},{8,40},{9,... | collective-permute-start | bytes 392 | tf_op jit(solution)/shard_map/ppermute | solution.py:37
  235.5 8.5 %collective-permute-start.21 = (f32[32]{0:T(128)S(1)}, f32[32]{0:T(128)S(1)}, u32[]{:S(2)}, u32[]{:S(2)}) collective-permute-start(f32[32]{0:T(128)S(1)} %add.509), channel_id=1, source_target_pairs={{0,32},{1,33},{2,34},{3,35},{4,36},{5,37},{6,38},{7,39},{8,40},{9,... | collective-permute-start | bytes 392 | tf_op jit(solution)/shard_map/ppermute | solution.py:37
  238.7 9.8 %collective-permute-start.6 = (f32[32]{0:T(128)S(1)}, f32[32]{0:T(128)S(1)}, u32[]{:S(2)}, u32[]{:S(2)}) collective-permute-start(f32[32]{0:T(128)S(1)} %add.474), channel_id=1, source_target_pairs={{0,64},{1,65},{2,66},{3,67},{4,68},{5,69},{6,70},{7,71},{8,72},{9,... | collective-permute-start | bytes 392 | tf_op jit(solution)/shard_map/ppermute | solution.py:37
  244.0 9.3 %collective-permute-start.22 = (f32[32]{0:T(128)S(1)}, f32[32]{0:T(128)S(1)}, u32[]{:S(2)}, u32[]{:S(2)}) collective-permute-start(f32[32]{0:T(128)S(1)} %add.510), channel_id=1, source_target_pairs={{0,64},{1,65},{2,66},{3,67},{4,68},{5,69},{6,70},{7,71},{8,72},{9,... | collective-permute-start | bytes 392 | tf_op jit(solution)/shard_map/ppermute | solution.py:37
  248.5 7.9 %collective-permute-start.7 = (f32[32]{0:T(128)S(1)}, f32[32]{0:T(128)S(1)}, u32[]{:S(2)}, u32[]{:S(2)}) collective-permute-start(f32[32]{0:T(128)S(1)} %add.475), channel_id=1, source_target_pairs={{0,128},{1,129},{2,130},{3,131},{4,132},{5,133},{6,134},{7,135},{8... | collective-permute-start | bytes 392 | tf_op jit(solution)/shard_map/ppermute | solution.py:37
  253.4 7.7 %collective-permute-start.23 = (f32[32]{0:T(128)S(1)}, f32[32]{0:T(128)S(1)}, u32[]{:S(2)}, u32[]{:S(2)}) collective-permute-start(f32[32]{0:T(128)S(1)} %add.511), channel_id=1, source_target_pairs={{0,128},{1,129},{2,130},{3,131},{4,132},{5,133},{6,134},{7,135},{8... | collective-permute-start | bytes 392 | tf_op jit(solution)/shard_map/ppermute | solution.py:37
  256.5 7.4 %collective-permute-start.8 = (f32[32]{0:T(128)S(1)}, f32[32]{0:T(128)S(1)}, u32[]{:S(2)}, u32[]{:S(2)}) collective-permute-start(f32[32]{0:T(128)S(1)} %add.476), channel_id=1, source_target_pairs={{0,256},{1,257},{2,258},{3,259},{4,260},{5,261},{6,262},{7,263},{8... | collective-permute-start | bytes 392 | tf_op jit(solution)/shard_map/ppermute | solution.py:37
  261.1 6.9 %collective-permute-start.24 = (f32[32]{0:T(128)S(1)}, f32[32]{0:T(128)S(1)}, u32[]{:S(2)}, u32[]{:S(2)}) collective-permute-start(f32[32]{0:T(128)S(1)} %add.512), channel_id=1, source_target_pairs={{0,256},{1,257},{2,258},{3,259},{4,260},{5,261},{6,262},{7,263},{8... | collective-permute-start | bytes 392 | tf_op jit(solution)/shard_map/ppermute | solution.py:37
  276.6 6.3 %collective-permute-start.27 = (f32[32]{0:T(128)S(1)}, f32[32]{0:T(128)S(1)}, u32[]{:S(2)}, u32[]{:S(2)}) collective-permute-start(f32[32]{0:T(128)S(1)} %add.515), channel_id=1, source_target_pairs={{0,4},{1,5},{2,6},{3,7},{4,0},{5,1},{6,2},{7,3},{8,12},{9,13},{10,... | collective-permute-start | bytes 392 | tf_op jit(solution)/shard_map/ppermute | solution.py:37
  283.0 9.3 %collective-permute-start.28 = (f32[32]{0:T(128)S(1)}, f32[32]{0:T(128)S(1)}, u32[]{:S(2)}, u32[]{:S(2)}) collective-permute-start(f32[32]{0:T(128)S(1)} %add.516), channel_id=1, source_target_pairs={{0,8},{1,9},{2,10},{3,11},{4,12},{5,13},{6,14},{7,15},{8,0},{9,1},... | collective-permute-start | bytes 392 | tf_op jit(solution)/shard_map/ppermute | solution.py:37
  297.7 6.3 %collective-permute-start.30 = (f32[32]{0:T(128)S(1)}, f32[32]{0:T(128)S(1)}, u32[]{:S(2)}, u32[]{:S(2)}) collective-permute-start(f32[32]{0:T(128)S(1)} %add.518), channel_id=1, source_target_pairs={{0,32},{1,33},{2,34},{3,35},{4,36},{5,37},{6,38},{7,39},{8,40},{9,... | collective-permute-start | bytes 392 | tf_op jit(solution)/shard_map/ppermute | solution.py:37
  304.1 9.3 %collective-permute-start.31 = (f32[32]{0:T(128)S(1)}, f32[32]{0:T(128)S(1)}, u32[]{:S(2)}, u32[]{:S(2)}) collective-permute-start(f32[32]{0:T(128)S(1)} %add.519), channel_id=1, source_target_pairs={{0,64},{1,65},{2,66},{3,67},{4,68},{5,69},{6,70},{7,71},{8,72},{9,... | collective-permute-start | bytes 392 | tf_op jit(solution)/shard_map/ppermute | solution.py:37
  318.8 6.9 %collective-permute-start.33 = (f32[32]{0:T(128)S(1)}, f32[32]{0:T(128)S(1)}, u32[]{:S(2)}, u32[]{:S(2)}) collective-permute-start(f32[32]{0:T(128)S(1)} %add.521), channel_id=1, source_target_pairs={{0,256},{1,257},{2,258},{3,259},{4,260},{5,261},{6,262},{7,263},{8... | collective-permute-start | bytes 392 | tf_op jit(solution)/shard_map/ppermute | solution.py:37
  325.8 7.3 %collective-permute-start.36 = (bf16[1,32,512]{2,1,0:T(8,128)(2,1)S(1)}, bf16[1,32,512]{2,1,0:T(8,128)(2,1)S(1)}, u32[]{:S(2)}, u32[]{:S(2)}) collective-permute-start(bf16[1,32,512]{2,1,0:T(8,128)(2,1)S(1)} %multiply_convert_fusion.3), channel_id=1, source_target_pairs={{0,256},{16,272},{32,288},{48,304},{64,320},{80,336},{96,352},{112... | collective-permute-start | bytes 98312 | tf_op jit(solution)/shard_map/ppermute | solution.py:50
  339.4 11.7 %collective-permute-start.38 = (bf16[4,32,512]{2,1,0:T(8,128)(2,1)S(1)}, bf16[4,32,512]{2,1,0:T(8,128)(2,1)S(1)}, u32[]{:S(2)}, u32[]{:S(2)}) collective-permute-start(bf16[4,32,512]{2,1,0:T(8,128)(2,1)S(1)} %maximum_select_fusion.18), channel_id=1, source_target_pairs={{0,64},{16,80},{32,96},{48,112},{64,0},{80,16},{96,32},{112,48},{1... | collective-permute-start | bytes 393224 | tf_op jit(solution)/shard_map/ppermute | solution.py:50
  351.1 16.6 %collective-permute-start.39 = (bf16[8,32,512]{2,1,0:T(8,128)(2,1)S(1)}, bf16[8,32,512]{2,1,0:T(8,128)(2,1)S(1)}, u32[]{:S(2)}, u32[]{:S(2)}) collective-permute-start(bf16[8,32,512]{2,1,0:T(8,128)(2,1)S(1)} %maximum_select_fusion.12), channel_id=1, source_target_pairs={{0,32},{16,48},{32,0},{48,16},{64,96},{80,112},{96,64},{112,80},{1... | collective-permute-start | bytes 786440 | tf_op jit(solution)/shard_map/ppermute | solution.py:50
  356.4 9.8 %collective-permute-start.34 = (bf16[32,64]{1,0:T(8,128)(2,1)S(1)}, bf16[32,64]{1,0:T(8,128)(2,1)S(1)}, u32[]{:S(2)}, u32[]{:S(2)}) collective-permute-start(bf16[32,64]{1,0:T(8,128)(2,1)S(1)} %get-tuple-element.27), channel_id=1, source_target_pairs={{0,1},{1,2},{2,3},{3,4},{4,5},{5,6},{6,7},{7,8},{8,9},{9,10},{10,1... | collective-permute-start | bytes 12296 | tf_op jit(solution)/shard_map/ppermute | solution.py:24
  358.3 9.2 %collective-permute-start.35 = (bf16[32,64]{1,0:T(8,128)(2,1)S(1)}, bf16[32,64]{1,0:T(8,128)(2,1)S(1)}, u32[]{:S(2)}, u32[]{:S(2)}) collective-permute-start(bf16[32,64]{1,0:T(8,128)(2,1)S(1)} %get-tuple-element.28), channel_id=1, source_target_pairs={{1,0},{2,1},{3,2},{4,3},{5,4},{6,5},{7,6},{8,7},{9,8},{10,9},{11,1... | collective-permute-start | bytes 12296 | tf_op jit(solution)/shard_map/ppermute | solution.py:26
  367.7 12.6 %collective-permute-start.40 = (bf16[16,32,512]{2,1,0:T(8,128)(2,1)S(1)}, bf16[16,32,512]{2,1,0:T(8,128)(2,1)S(1)}, u32[]{:S(2)}, u32[]{:S(2)}) collective-permute-start(bf16[16,32,512]{2,1,0:T(8,128)(2,1)S(1)} %maximum_select_fusion.6), channel_id=1, source_target_pairs={{0,16},{16,0},{32,48},{48,32},{64,80},{80,64},{96,112},{112,96},{1... | collective-permute-start | bytes 1572872 | tf_op jit(solution)/shard_map/ppermute | solution.py:50
  394.4 6.3 %collective-permute-start.43 = (f32[32]{0:T(128)S(1)}, f32[32]{0:T(128)S(1)}, u32[]{:S(2)}, u32[]{:S(2)}) collective-permute-start(f32[32]{0:T(128)S(1)} %add.532), channel_id=1, source_target_pairs={{0,4},{1,5},{2,6},{3,7},{4,0},{5,1},{6,2},{7,3},{8,12},{9,13},{10,... | collective-permute-start | bytes 392 | tf_op jit(solution)/shard_map/ppermute | solution.py:37
  400.7 9.3 %collective-permute-start.44 = (f32[32]{0:T(128)S(1)}, f32[32]{0:T(128)S(1)}, u32[]{:S(2)}, u32[]{:S(2)}) collective-permute-start(f32[32]{0:T(128)S(1)} %add.533), channel_id=1, source_target_pairs={{0,8},{1,9},{2,10},{3,11},{4,12},{5,13},{6,14},{7,15},{8,0},{9,1},... | collective-permute-start | bytes 392 | tf_op jit(solution)/shard_map/ppermute | solution.py:37
  421.8 9.3 %collective-permute-start.47 = (f32[32]{0:T(128)S(1)}, f32[32]{0:T(128)S(1)}, u32[]{:S(2)}, u32[]{:S(2)}) collective-permute-start(f32[32]{0:T(128)S(1)} %add.536), channel_id=1, source_target_pairs={{0,64},{1,65},{2,66},{3,67},{4,68},{5,69},{6,70},{7,71},{8,72},{9,... | collective-permute-start | bytes 392 | tf_op jit(solution)/shard_map/ppermute | solution.py:37
  436.5 6.9 %collective-permute-start.49 = (f32[32]{0:T(128)S(1)}, f32[32]{0:T(128)S(1)}, u32[]{:S(2)}, u32[]{:S(2)}) collective-permute-start(f32[32]{0:T(128)S(1)} %add.538), channel_id=1, source_target_pairs={{0,256},{1,257},{2,258},{3,259},{4,260},{5,261},{6,262},{7,263},{8... | collective-permute-start | bytes 392 | tf_op jit(solution)/shard_map/ppermute | solution.py:37
  458.5 9.3 %collective-permute-start.53 = (f32[32]{0:T(128)S(1)}, f32[32]{0:T(128)S(1)}, u32[]{:S(2)}, u32[]{:S(2)}) collective-permute-start(f32[32]{0:T(128)S(1)} %add.543), channel_id=1, source_target_pairs={{0,8},{1,9},{2,10},{3,11},{4,12},{5,13},{6,14},{7,15},{8,0},{9,1},... | collective-permute-start | bytes 392 | tf_op jit(solution)/shard_map/ppermute | solution.py:37
  479.5 9.3 %collective-permute-start.56 = (f32[32]{0:T(128)S(1)}, f32[32]{0:T(128)S(1)}, u32[]{:S(2)}, u32[]{:S(2)}) collective-permute-start(f32[32]{0:T(128)S(1)} %add.546), channel_id=1, source_target_pairs={{0,64},{1,65},{2,66},{3,67},{4,68},{5,69},{6,70},{7,71},{8,72},{9,... | collective-permute-start | bytes 392 | tf_op jit(solution)/shard_map/ppermute | solution.py:37
  494.3 6.9 %collective-permute-start.58 = (f32[32]{0:T(128)S(1)}, f32[32]{0:T(128)S(1)}, u32[]{:S(2)}, u32[]{:S(2)}) collective-permute-start(f32[32]{0:T(128)S(1)} %add.548), channel_id=1, source_target_pairs={{0,256},{1,257},{2,258},{3,259},{4,260},{5,261},{6,262},{7,263},{8... | collective-permute-start | bytes 392 | tf_op jit(solution)/shard_map/ppermute | solution.py:37
  501.3 7.3 %collective-permute-start.61 = (bf16[1,32,512]{2,1,0:T(8,128)(2,1)S(1)}, bf16[1,32,512]{2,1,0:T(8,128)(2,1)S(1)}, u32[]{:S(2)}, u32[]{:S(2)}) collective-permute-start(bf16[1,32,512]{2,1,0:T(8,128)(2,1)S(1)} %multiply_convert_fusion.1), channel_id=1, source_target_pairs={{0,256},{16,272},{32,288},{48,304},{64,320},{80,336},{96,352},{112... | collective-permute-start | bytes 98312 | tf_op jit(solution)/shard_map/ppermute | solution.py:50
  514.8 11.1 %collective-permute-start.63 = (bf16[4,32,512]{2,1,0:T(8,128)(2,1)S(1)}, bf16[4,32,512]{2,1,0:T(8,128)(2,1)S(1)}, u32[]{:S(2)}, u32[]{:S(2)}) collective-permute-start(bf16[4,32,512]{2,1,0:T(8,128)(2,1)S(1)} %maximum_select_fusion.20), channel_id=1, source_target_pairs={{0,64},{16,80},{32,96},{48,112},{64,0},{80,16},{96,32},{112,48},{1... | collective-permute-start | bytes 393224 | tf_op jit(solution)/shard_map/ppermute | solution.py:50
  526.0 16.1 %collective-permute-start.64 = (bf16[8,32,512]{2,1,0:T(8,128)(2,1)S(1)}, bf16[8,32,512]{2,1,0:T(8,128)(2,1)S(1)}, u32[]{:S(2)}, u32[]{:S(2)}) collective-permute-start(bf16[8,32,512]{2,1,0:T(8,128)(2,1)S(1)} %maximum_select_fusion.14), channel_id=1, source_target_pairs={{0,32},{16,48},{32,0},{48,16},{64,96},{80,112},{96,64},{112,80},{1... | collective-permute-start | bytes 786440 | tf_op jit(solution)/shard_map/ppermute | solution.py:50
  530.8 9.8 %collective-permute-start.59 = (bf16[32,64]{1,0:T(8,128)(2,1)S(1)}, bf16[32,64]{1,0:T(8,128)(2,1)S(1)}, u32[]{:S(2)}, u32[]{:S(2)}) collective-permute-start(bf16[32,64]{1,0:T(8,128)(2,1)S(1)} %get-tuple-element.21), channel_id=1, source_target_pairs={{0,1},{1,2},{2,3},{3,4},{4,5},{5,6},{6,7},{7,8},{8,9},{9,10},{10,1... | collective-permute-start | bytes 12296 | tf_op jit(solution)/shard_map/ppermute | solution.py:24
  532.8 9.2 %collective-permute-start.60 = (bf16[32,64]{1,0:T(8,128)(2,1)S(1)}, bf16[32,64]{1,0:T(8,128)(2,1)S(1)}, u32[]{:S(2)}, u32[]{:S(2)}) collective-permute-start(bf16[32,64]{1,0:T(8,128)(2,1)S(1)} %get-tuple-element.22), channel_id=1, source_target_pairs={{1,0},{2,1},{3,2},{4,3},{5,4},{6,5},{7,6},{8,7},{9,8},{10,9},{11,1... | collective-permute-start | bytes 12296 | tf_op jit(solution)/shard_map/ppermute | solution.py:26
  542.2 11.1 %collective-permute-start.65 = (bf16[16,32,512]{2,1,0:T(8,128)(2,1)S(1)}, bf16[16,32,512]{2,1,0:T(8,128)(2,1)S(1)}, u32[]{:S(2)}, u32[]{:S(2)}) collective-permute-start(bf16[16,32,512]{2,1,0:T(8,128)(2,1)S(1)} %maximum_select_fusion.8), channel_id=1, source_target_pairs={{0,16},{16,0},{32,48},{48,32},{64,80},{80,64},{96,112},{112,96},{1... | collective-permute-start | bytes 1572872 | tf_op jit(solution)/shard_map/ppermute | solution.py:50
  573.6 9.3 %collective-permute-start.69 = (f32[32]{0:T(128)S(1)}, f32[32]{0:T(128)S(1)}, u32[]{:S(2)}, u32[]{:S(2)}) collective-permute-start(f32[32]{0:T(128)S(1)} %add.560), channel_id=1, source_target_pairs={{0,8},{1,9},{2,10},{3,11},{4,12},{5,13},{6,14},{7,15},{8,0},{9,1},... | collective-permute-start | bytes 392 | tf_op jit(solution)/shard_map/ppermute | solution.py:37
  594.7 9.3 %collective-permute-start.72 = (f32[32]{0:T(128)S(1)}, f32[32]{0:T(128)S(1)}, u32[]{:S(2)}, u32[]{:S(2)}) collective-permute-start(f32[32]{0:T(128)S(1)} %add.563), channel_id=1, source_target_pairs={{0,64},{1,65},{2,66},{3,67},{4,68},{5,69},{6,70},{7,71},{8,72},{9,... | collective-permute-start | bytes 392 | tf_op jit(solution)/shard_map/ppermute | solution.py:37
  609.5 6.9 %collective-permute-start.74 = (f32[32]{0:T(128)S(1)}, f32[32]{0:T(128)S(1)}, u32[]{:S(2)}, u32[]{:S(2)}) collective-permute-start(f32[32]{0:T(128)S(1)} %add.565), channel_id=1, source_target_pairs={{0,256},{1,257},{2,258},{3,259},{4,260},{5,261},{6,262},{7,263},{8... | collective-permute-start | bytes 392 | tf_op jit(solution)/shard_map/ppermute | solution.py:37
  (32 other events, 232.0 us)
Sparse Core Ops, SparseCore 0:
  10.5 106.1 all-gather.1

commit v2 on v0

--- a/solution.py
+++ b/solution.py
@@ -28,6 +28,19 @@
             axis=dim,
         )
     return cells
+
+
+def total_over_devices(values):
+    count = lax.axis_size("band") * lax.axis_size("seq")
+    spread = jnp.broadcast_to(values[None], (count,) + values.shape)
+    rows = lax.all_to_all(spread, ("band", "seq"), split_axis=0, concat_axis=0, tiled=True)
+    return jnp.sum(rows, axis=0)
+
+
+def band_gather(block):
+    count = lax.axis_size("band")
+    spread = jnp.broadcast_to(block[None], (count,) + block.shape)
+    return lax.all_to_all(spread, "band", split_axis=0, concat_axis=0, tiled=True)
 
 
 def on_device(posteriors, seed_mask, frame_perm, lengths, embeddings, partners, levels):
@@ -62,7 +75,7 @@
         linked, jnp.exp(-offset.astype(jnp.float32) / decay_len), jnp.float32(0.0)
     ).astype(jnp.bfloat16)
     near_degree = jnp.sum(band_tiles.astype(jnp.float32), axis=1).reshape(frames)
-    gathered = lax.all_gather(embeddings, "band", axis=0, tiled=True)
+    gathered = band_gather(embeddings)
     embed_width = embeddings.shape[1]
     partner_rows = gathered.reshape(-1, 128, embed_width)[partners]
     own_rows = embeddings.reshape(tile_count, 128, embed_width)
@@ -79,12 +92,12 @@
     norm_scale = 1.0 / jnp.sqrt(near_degree + far_degree)
 
     def squares(residual):
-        return lax.psum(jnp.sum(residual * residual, axis=1), ("band", "seq"))
+        return total_over_devices(jnp.sum(residual * residual, axis=1))
 
     solution = jnp.zeros((channels, frames), jnp.float32)
     residual = labels
     direction = labels
-    norm_now = squares(residual)
+    first_norm = jnp.sum(residual * residual, axis=1)
     for iteration in range(ITERS):
         lifted = (norm_scale[None, :] * direction).astype(jnp.bfloat16)
         padded = with_halo(lifted, ((("band", "seq"), 1),), RADIUS)
@@ -95,13 +108,18 @@
         near_term = jnp.einsum(
             "tcw,twa->cta", windows, band_tiles, preferred_element_type=jnp.float32
         ).reshape(channels, frames)
-        spread = lax.all_gather(lifted, "band", axis=1, tiled=True).reshape(channels, -1, 128)
+        spread = jnp.transpose(band_gather(lifted), (1, 0, 2)).reshape(channels, -1, 128)
         far_tiles = spread[:, partners]
         far_term = jnp.einsum(
             "ctkj,tkji->cti", far_tiles, affinity, preferred_element_type=jnp.float32
         ).reshape(channels, frames)
         image = direction - spread_rate * norm_scale[None, :] * (near_term + far_term)
-        curve = lax.psum(jnp.sum(direction * image, axis=1), ("band", "seq"))
+        curve = jnp.sum(direction * image, axis=1)
+        if iteration == 0:
+            both = total_over_devices(jnp.stack([first_norm, curve]))
+            norm_now, curve = both[0], both[1]
+        else:
+            curve = total_over_devices(curve)
         alpha = norm_now / curve
         solution = solution + alpha[:, None] * direction
         residual = residual - alpha[:, None] * image

time: 864 us -> 530 us (0.61)
  blocking collectives: 479 us -> 160 us
  waiting for transfers between devices: 260 us -> 210 us
  starting transfers between devices: 39.9 us -> 67.2 us
  between operations: 13.5 us -> 0.99 us
    psum x5 -> x0, blocking collectives: 479 us -> none  [the longest x3 287 us: squares(): return lax.psum(jnp.sum(residual * residual, axis=1), ('band', 'seq'))]
    all_gather x4 -> x0, waiting for transfers between devices: 256 us -> none  [the longest x3 180 us: on_device(): lax.all_gather(lifted, 'band', axis=1, tiled=True)]
    all_to_all x1 -> x4, waiting for transfers between devices: 0.01 us -> 173 us  [band_gather(): lax.all_to_all(spread, 'band', split_axis=0, concat_axis=0, tiled=True)]
    all_to_all x0 -> x6, blocking collectives: none -> 160 us  [the longest x5 142 us: total_over_devices(): lax.all_to_all(spread, ('band', 'seq'), split_axis=0, concat_axis=0, tile...]
    ppermute x3, waiting for transfers between devices: 0.01 us -> 36.3 us  [with_halo(): lax.ppermute(tail, axis, [(i, (i + 1) % count) for i in range(ends)])]
    all_to_all x1 -> x4, starting transfers between devices: 10.2 us -> 32.5 us  [band_gather(): lax.all_to_all(spread, 'band', split_axis=0, concat_axis=0, tiled=True)]
    broadcast_in_dim x0 -> x9, local copies, waits for them, and re-layouts: none -> 9.11 us  [the longest x4 8.41 us: band_gather(): spread = jnp.broadcast_to(block[None], (count,) + block.shape)]
  transfers between devices with their start and end apart: 11 -> 10, of which waited for: 7 -> 6; matrix products, arithmetic and copies ran while one was open for 3% -> 4% of each run, Pallas kernels for 0% -> 0%
where the time goes in v2:
time: 530 us; the launch traced here: 520 us
  waiting for transfers between devices  210 us (40%)
  blocking collectives  160 us (30%)
  starting transfers between devices  67.2 us (13%)
  local copies, waits for them, and re-layouts  44.6 us (8%)
  matrix products  20 us (4%)
  other arithmetic  17.3 us (3%)
    all_to_all x4, waiting for transfers between devices, band_gather(): lax.all_to_all(spread, 'band', split_axis=0, concat_axis=0, tiled=True)  173 us
    all_to_all x5, blocking collectives, total_over_devices(): lax.all_to_all(spread, ('band', 'seq'), split_axis=0, concat_axis=0, tile...  142 us
    ppermute x3, waiting for transfers between devices, with_halo(): lax.ppermute(tail, axis, [(i, (i + 1) % count) for i in range(ends)])  36.3 us
    all_to_all x4, starting transfers between devices, band_gather(): lax.all_to_all(spread, 'band', split_axis=0, concat_axis=0, tiled=True)  32.5 us
    ppermute x3, starting transfers between devices, with_halo(): lax.ppermute(head, axis, [((i + 1) % count, i) for i in range(ends)])  28.9 us
    all_to_all x1, blocking collectives, on_device(): lax.all_to_all(ordered, 'band', split_axis=1, concat_axis=1, tiled=True)  18.1 us
  transfers between devices with their start and end apart: 10, of which 6 were waited for; matrix products, arithmetic and copies ran while one was open for 4% of the time, Pallas kernels for 0%

profile of v2, /device:TPU:6, one launch (start us, length us, event | category | flops | bytes accessed | tf_op | source)
XLA Modules:
  0.0 519.9 jit_solution(15954365283802545551)
XLA Ops:
  0.7 0.8 broadcast_multiply_fusion
  2.8 1.3 reduce.15
  4.2 1.3 gather_fusion
  5.9 18.1 %all_to_all.54 = bf16[32,2,256]{2,1,0:T(2,128)(2,1)S(1)} all-to-all(bf16[32,2,256]{2,1,0:T(2,128)(2,1)S(1)} %reshape.758), channel_id=1, replica_groups=mesh['band'=32,'seq'=16] {'band'}, dimensions={0} | all-to-all | bytes 65536 | tf_op jit(solution)/shard_map/all_to_all | solution.py:55
  23.9 5.1 broadcast_in_dim.37
  29.1 6.9 %all-to-all-start.1 = ((bf16[32,512,256]{2,1,0:T(8,128)(2,1)}), bf16[32,512,256]{2,1,0:T(8,128)(2,1)}, u32[]{:S(2)}, u32[]{:S(2)}) async-start(bf16[32,512,256]{2,1,0:T(8,128)(2,1)} %broadcast_in_dim.37), calls=%async_computation.1 | async-start | bytes 16777216 | tf_op jit(solution)/shard_map/all_to_all | solution.py:43
  36.1 6.8 %gather_fusion.3 = pred[1024]{0:T(1024)(128)(4,1)S(1)} fusion(pred[640]{0:T(1024)(128)(4,1)S(1)} %compare_and_fusion.1, s32[1024]{0:T(1024)S(1)} %broadcast_clamp_fusion), kind=kCustom, calls=%fused_computation.3 | custom fusion | bytes 6144 | tf_op jit(solution)/shard_map/gather | solution.py:72
  43.8 4.5 gather_fusion.1
  48.4 2.3 gather_fusion.2
  51.8 165.6 %all-to-all-done.1 = bf16[32,512,256]{2,1,0:T(8,128)(2,1)} async-done(((bf16[32,512,256]{2,1,0:T(8,128)(2,1)}), bf16[32,512,256]{2,1,0:T(8,128)(2,1)}, u32[]{:S(2)}, u32[]{:S(2)}) %all-to-all-start.1) | async-done | bytes 8388640 | tf_op jit(solution)/shard_map/all_to_all | solution.py:43
  217.4 10.0 %gather_fusion.4 = bf16[128,128,256]{2,1,0:T(8,128)(2,1)} fusion(bf16[128,128,256]{2,1,0:T(8,128)(2,1)} %bitcast.9, s32[1024]{0:T(1024)S(1)} %pad_clamp_fusion), kind=kCustom, calls=%fused_computation.4 | custom fusion | bytes 16777728 | tf_op jit(solution)/shard_map/gather | solution.py:80
  227.5 7.7 %convert_reduce_fusion = (f32[4,128]{1,0:T(4,128)S(1)}, bf16[4,32,128,128]{3,2,1,0:T(8,128)(2,1)}) fusion(f32[4,32]{1,0:T(4,128)S(1)} %convert_multiply_fusion.3, bf16[4,32,128,256]{3,2,1,0:T(8,128)(2,1)} %bitcast.156, bf16[4,128,256,1]{2,1,3,0:T(8,128)(2,1)S(1)} %bitcast.170), kind=kOutput, calls=%fused_computation.8 | convolution fusion | flops 1086324224 | bytes 12847616 | tf_op jit(solution)/shard_map/tkje,tie->tkji/dot_general | solution.py:82
  235.7 1.1 broadcast_in_dim.39
  236.8 13.9 %all-to-all-start.2 = ((bf16[32,32,512]{2,1,0:T(8,128)(2,1)}), bf16[32,32,512]{2,1,0:T(8,128)(2,1)S(1)}, u32[]{:S(2)}, u32[]{:S(2)}) async-start(bf16[32,32,512]{2,1,0:T(8,128)(2,1)} %broadcast_in_dim.39), calls=%async_computation.2 | async-start | bytes 2097152 | tf_op jit(solution)/shard_map/all_to_all | solution.py:43
  250.8 1.9 collective-permute-start
  252.8 12.8 %collective-permute-start.1 = (bf16[32,64]{1,0:T(8,128)(2,1)S(1)}, bf16[32,64]{1,0:T(8,128)(2,1)S(1)}, u32[]{:S(2)}, u32[]{:S(2)}) collective-permute-start(bf16[32,64]{1,0:T(8,128)(2,1)S(1)} %get-tuple-element.28), channel_id=1, source_target_pairs={{1,0},{2,1},{3,2},{4,3},{5,4},{6,5},{7,6},{8,7},{9,8},{10,9},{11,1... | collective-permute-start | bytes 12296 | tf_op jit(solution)/shard_map/ppermute | solution.py:26
  265.7 13.7 %collective-permute-done = bf16[32,64]{1,0:T(8,128)(2,1)S(1)} collective-permute-done((bf16[32,64]{1,0:T(8,128)(2,1)S(1)}, bf16[32,64]{1,0:T(8,128)(2,1)S(1)}, u32[]{:S(2)}, u32[]{:S(2)}) %collective-permute-start) | collective-permute-done | bytes 4128 | tf_op jit(solution)/shard_map/ppermute | solution.py:24
  282.1 0.8 gather_fusion.5
  282.9 2.9 fusion.3
  286.3 35.6 %all_to_all.55 = f32[512,2,32]{2,1,0:T(2,128)S(1)} all-to-all(f32[512,2,32]{2,1,0:T(2,128)S(1)} %broadcast_in_dim.40), channel_id=1, replica_groups=mesh['band'=32,'seq'=16] {'band','seq'}, dimensions={0} | all-to-all | bytes 262144 | tf_op jit(solution)/shard_map/all_to_all | solution.py:36
  322.7 25.9 %all_to_all.56 = f32[512,1,32]{2,1,0:T(1,128)S(1)} all-to-all(f32[512,1,32]{2,1,0:T(1,128)S(1)} %broadcast_in_dim.41), channel_id=1, replica_groups=mesh['band'=32,'seq'=16] {'band','seq'}, dimensions={0} | all-to-all | bytes 131072 | tf_op jit(solution)/shard_map/all_to_all | solution.py:36
  349.2 0.9 multiply_convert_fusion.2
  350.1 1.1 broadcast_in_dim.42
  351.2 5.8 %all-to-all-start.5 = ((bf16[32,32,512]{2,1,0:T(8,128)(2,1)}), bf16[32,32,512]{2,1,0:T(8,128)(2,1)S(1)}, u32[]{:S(2)}, u32[]{:S(2)}) async-start(bf16[32,32,512]{2,1,0:T(8,128)(2,1)} %broadcast_in_dim.42), calls=%async_computation.5 | async-start | bytes 2097152 | tf_op jit(solution)/shard_map/all_to_all | solution.py:43
  357.2 1.9 collective-permute-start.2
  359.1 8.0 %collective-permute-start.3 = (bf16[32,64]{1,0:T(8,128)(2,1)S(1)}, bf16[32,64]{1,0:T(8,128)(2,1)S(1)}, u32[]{:S(2)}, u32[]{:S(2)}) collective-permute-start(bf16[32,64]{1,0:T(8,128)(2,1)S(1)} %get-tuple-element.22), channel_id=1, source_target_pairs={{1,0},{2,1},{3,2},{4,3},{5,4},{6,5},{7,6},{8,7},{9,8},{10,9},{11,1... | collective-permute-start | bytes 12296 | tf_op jit(solution)/shard_map/ppermute | solution.py:26
  367.1 11.3 %collective-permute-done.2 = bf16[32,64]{1,0:T(8,128)(2,1)S(1)} collective-permute-done((bf16[32,64]{1,0:T(8,128)(2,1)S(1)}, bf16[32,64]{1,0:T(8,128)(2,1)S(1)}, u32[]{:S(2)}, u32[]{:S(2)}) %collective-permute-start.2) | collective-permute-done | bytes 4128 | tf_op jit(solution)/shard_map/ppermute | solution.py:24
  378.6 1.4 fusion.14
  380.0 3.9 all-to-all-done.5
  385.9 0.9 gather_fusion.6
  386.8 2.9 fusion.2
  389.9 0.9 multiply_reduce_fusion.1
  390.9 27.4 %all_to_all.57 = f32[512,1,32]{2,1,0:T(1,128)S(1)} all-to-all(f32[512,1,32]{2,1,0:T(1,128)S(1)} %broadcast_in_dim.43), channel_id=1, replica_groups=mesh['band'=32,'seq'=16] {'band','seq'}, dimensions={0} | all-to-all | bytes 131072 | tf_op jit(solution)/shard_map/all_to_all | solution.py:36
  419.4 0.9 multiply_reduce_fusion
  420.5 26.0 %all_to_all.58 = f32[512,1,32]{2,1,0:T(1,128)S(1)} all-to-all(f32[512,1,32]{2,1,0:T(1,128)S(1)} %broadcast_in_dim.44), channel_id=1, replica_groups=mesh['band'=32,'seq'=16] {'band','seq'}, dimensions={0} | all-to-all | bytes 131072 | tf_op jit(solution)/shard_map/all_to_all | solution.py:36
  447.7 1.6 multiply_convert_fusion.1
  449.3 1.1 broadcast_in_dim.45
  450.4 5.8 %all-to-all-start.8 = ((bf16[32,32,512]{2,1,0:T(8,128)(2,1)}), bf16[32,32,512]{2,1,0:T(8,128)(2,1)S(1)}, u32[]{:S(2)}, u32[]{:S(2)}) async-start(bf16[32,32,512]{2,1,0:T(8,128)(2,1)} %broadcast_in_dim.45), calls=%async_computation.8 | async-start | bytes 2097152 | tf_op jit(solution)/shard_map/all_to_all | solution.py:43
  456.3 1.9 collective-permute-start.4
  458.2 8.1 %collective-permute-start.5 = (bf16[32,64]{1,0:T(8,128)(2,1)S(1)}, bf16[32,64]{1,0:T(8,128)(2,1)S(1)}, u32[]{:S(2)}, u32[]{:S(2)}) collective-permute-start(bf16[32,64]{1,0:T(8,128)(2,1)S(1)} %get-tuple-element.16), channel_id=1, source_target_pairs={{1,0},{2,1},{3,2},{4,3},{5,4},{6,5},{7,6},{8,7},{9,8},{10,9},{11,1... | collective-permute-start | bytes 12296 | tf_op jit(solution)/shard_map/ppermute | solution.py:26
  466.3 11.3 %collective-permute-done.4 = bf16[32,64]{1,0:T(8,128)(2,1)S(1)} collective-permute-done((bf16[32,64]{1,0:T(8,128)(2,1)S(1)}, bf16[32,64]{1,0:T(8,128)(2,1)S(1)}, u32[]{:S(2)}, u32[]{:S(2)}) %collective-permute-start.4) | collective-permute-done | bytes 4128 | tf_op jit(solution)/shard_map/ppermute | solution.py:24
  477.8 1.4 fusion.15
  479.2 3.9 all-to-all-done.8
  485.1 0.9 gather_fusion.7
  485.9 2.9 fusion.1
  489.0 0.9 fusion.12
  490.1 27.4 %all_to_all.59 = f32[512,1,32]{2,1,0:T(1,128)S(1)} all-to-all(f32[512,1,32]{2,1,0:T(1,128)S(1)} %broadcast_in_dim.46), channel_id=1, replica_groups=mesh['band'=32,'seq'=16] {'band','seq'}, dimensions={0} | all-to-all | bytes 131072 | tf_op jit(solution)/shard_map/all_to_all | solution.py:36
  518.1 1.6 multiply_add_fusion
  (144 shorter events, 17.6 us)
Async XLA Ops:
  29.0 13.9 %copy-start.25 = (s32[256]{0:T(256)S(1)}, s32[256]{0:T(256)}, u32[]{:S(2)}) copy-start(s32[256]{0:T(256)} %param.10) | copy-start | bytes 3076
  29.0 21.7 %copy-start.20 = (s32[4,32]{1,0:T(4,128)S(1)}, s32[4,32]{1,0:T(4,128)}, u32[]{:S(2)}) copy-start(s32[4,32]{1,0:T(4,128)} %param.12) | copy-start | bytes 1540
  29.0 22.5 %copy-start.21 = (s32[4,32]{1,0:T(4,128)S(1)}, s32[4,32]{1,0:T(4,128)}, u32[]{:S(2)}) copy-start(s32[4,32]{1,0:T(4,128)} %param.13) | copy-start | bytes 1540
  29.1 188.4 %all-to-all-start.1 = ((bf16[32,512,256]{2,1,0:T(8,128)(2,1)}), bf16[32,512,256]{2,1,0:T(8,128)(2,1)}, u32[]{:S(2)}, u32[]{:S(2)}) async-start(bf16[32,512,256]{2,1,0:T(8,128)(2,1)} %broadcast_in_dim.37), calls=%async_computation.1 | async-start | bytes 16777216 | tf_op jit(solution)/shard_map/all_to_all | solution.py:43
  42.9 236.6 %copy-start.26 = (pred[4,256]{1,0:T(4,128)(4,1)}, pred[4,256]{1,0:T(4,128)(4,1)S(1)}, u32[]{:S(2)}) copy-start(pred[4,256]{1,0:T(4,128)(4,1)S(1)} %and.33) | copy-start | bytes 3076
  50.7 228.8 %copy-start.22 = (s32[512]{0:T(512)}, s32[512]{0:T(512)S(1)}, u32[]{:S(2)}) copy-start(s32[512]{0:T(512)S(1)} %gather_fusion.2) | copy-start | bytes 6148
  50.7 228.7 %copy-start.13 = (s32[4,256]{1,0:T(4,128)}, s32[4,256]{1,0:T(4,128)S(1)}, u32[]{:S(2)}) copy-start(s32[4,256]{1,0:T(4,128)S(1)} %eq.17) | copy-start | bytes 12292
  50.9 231.2 %copy-start.5 = (s32[1024]{0:T(1024)}, s32[1024]{0:T(1024)S(1)}, u32[]{:S(2)}) copy-start(s32[1024]{0:T(1024)S(1)} %pad_clamp_fusion) | copy-start | bytes 12292
  50.9 228.6 %copy-start.17 = (s32[4,128]{1,0:T(4,128)}, s32[4,128]{1,0:T(4,128)S(1)}, u32[]{:S(2)}) copy-start(s32[4,128]{1,0:T(4,128)S(1)} %iota_add_fusion.2) | copy-start | bytes 6148
  51.0 228.5 %copy-start.10 = (s32[4,256]{1,0:T(4,128)}, s32[4,256]{1,0:T(4,128)S(1)}, u32[]{:S(2)}) copy-start(s32[4,256]{1,0:T(4,128)S(1)} %iota_add_fusion.1) | copy-start | bytes 12292
  51.8 183.9 %copy-start.3 = (f32[32,512]{1,0:T(8,128)}, f32[32,512]{1,0:T(8,128)S(1)}, u32[]{:S(2)}) copy-start(f32[32,512]{1,0:T(8,128)S(1)} %copy.83) | copy-start | bytes 196612
  217.4 10.0 %copy-start.4 = (bf16[512,256]{1,0:T(8,128)(2,1)S(1)}, bf16[512,256]{1,0:T(8,128)(2,1)}, u32[]{:S(2)}) copy-start(bf16[512,256]{1,0:T(8,128)(2,1)} %param.11) | copy-start | bytes 786436
  235.7 50.1 %copy-start.6 = (f32[512]{0:T(512)}, f32[512]{0:T(512)S(1)}, u32[]{:S(2)}) copy-start(f32[512]{0:T(512)S(1)} %get-tuple-element.10) | copy-start | bytes 6148
  236.8 43.3 %all-to-all-start.2 = ((bf16[32,32,512]{2,1,0:T(8,128)(2,1)}), bf16[32,32,512]{2,1,0:T(8,128)(2,1)S(1)}, u32[]{:S(2)}, u32[]{:S(2)}) async-start(bf16[32,32,512]{2,1,0:T(8,128)(2,1)} %broadcast_in_dim.39), calls=%async_computation.2 | async-start | bytes 2097152 | tf_op jit(solution)/shard_map/all_to_all | solution.py:43
  250.8 28.5 %collective-permute-start = (bf16[32,64]{1,0:T(8,128)(2,1)S(1)}, bf16[32,64]{1,0:T(8,128)(2,1)S(1)}, u32[]{:S(2)}, u32[]{:S(2)}) collective-permute-start(bf16[32,64]{1,0:T(8,128)(2,1)S(1)} %get-tuple-element.27), channel_id=1, source_target_pairs={{0,1},{1,2},{2,3},{3,4},{4,5},{5,6},{6,7},{7,8},{8,9},{9,10},{10,1... | collective-permute-start | bytes 12296 | tf_op jit(solution)/shard_map/ppermute | solution.py:24
  252.8 26.6 %collective-permute-start.1 = (bf16[32,64]{1,0:T(8,128)(2,1)S(1)}, bf16[32,64]{1,0:T(8,128)(2,1)S(1)}, u32[]{:S(2)}, u32[]{:S(2)}) collective-permute-start(bf16[32,64]{1,0:T(8,128)(2,1)S(1)} %get-tuple-element.28), channel_id=1, source_target_pairs={{1,0},{2,1},{3,2},{4,3},{5,4},{6,5},{7,6},{8,7},{9,8},{10,9},{11,1... | collective-permute-start | bytes 12296 | tf_op jit(solution)/shard_map/ppermute | solution.py:26
  282.1 96.4 %copy-start.11 = (s32[4,256]{1,0:T(4,128)S(1)}, s32[4,256]{1,0:T(4,128)}, u32[]{:S(2)}) copy-start(s32[4,256]{1,0:T(4,128)} %copy-done.10) | copy-start | bytes 12292
  282.1 96.4 %copy-start.14 = (s32[4,256]{1,0:T(4,128)S(1)}, s32[4,256]{1,0:T(4,128)}, u32[]{:S(2)}) copy-start(s32[4,256]{1,0:T(4,128)} %copy-done.13) | copy-start | bytes 12292
  282.1 96.4 %copy-start.18 = (s32[4,128]{1,0:T(4,128)S(1)}, s32[4,128]{1,0:T(4,128)}, u32[]{:S(2)}) copy-start(s32[4,128]{1,0:T(4,128)} %copy-done.17) | copy-start | bytes 6148
  282.1 96.4 %copy-start.23 = (s32[512]{0:T(512)S(1)}, s32[512]{0:T(512)}, u32[]{:S(2)}) copy-start(s32[512]{0:T(512)} %copy-done.22) | copy-start | bytes 6148
  282.1 96.4 %copy-start.27 = (pred[4,256]{1,0:T(4,128)(4,1)S(1)}, pred[4,256]{1,0:T(4,128)(4,1)}, u32[]{:S(2)}) copy-start(pred[4,256]{1,0:T(4,128)(4,1)} %copy-done.26) | copy-start | bytes 3076
  285.9 65.4 %copy-start.2 = (f32[4,128,32]{1,2,0:T(8,128)}, f32[4,128,32]{1,2,0:T(8,128)S(1)}, u32[]{:S(2)}) copy-start(f32[4,128,32]{1,2,0:T(8,128)S(1)} %fusion.3) | copy-start | bytes 196612
  322.4 28.8 %copy-start.7 = (f32[32]{0:T(128)}, f32[32]{0:T(128)S(1)}, u32[]{:S(2)}) copy-start(f32[32]{0:T(128)S(1)} %bitcast_divide_fusion) | copy-start | bytes 388
  349.2 2.1 copy-start.31
  349.2 2.0 copy-start.8
  351.2 32.7 %all-to-all-start.5 = ((bf16[32,32,512]{2,1,0:T(8,128)(2,1)}), bf16[32,32,512]{2,1,0:T(8,128)(2,1)S(1)}, u32[]{:S(2)}, u32[]{:S(2)}) async-start(bf16[32,32,512]{2,1,0:T(8,128)(2,1)} %broadcast_in_dim.42), calls=%async_computation.5 | async-start | bytes 2097152 | tf_op jit(solution)/shard_map/all_to_all | solution.py:43
  357.2 21.3 %collective-permute-start.2 = (bf16[32,64]{1,0:T(8,128)(2,1)S(1)}, bf16[32,64]{1,0:T(8,128)(2,1)S(1)}, u32[]{:S(2)}, u32[]{:S(2)}) collective-permute-start(bf16[32,64]{1,0:T(8,128)(2,1)S(1)} %get-tuple-element.21), channel_id=1, source_target_pairs={{0,1},{1,2},{2,3},{3,4},{4,5},{5,6},{6,7},{7,8},{8,9},{9,10},{10,1... | collective-permute-start | bytes 12296 | tf_op jit(solution)/shard_map/ppermute | solution.py:24
  359.1 19.4 %collective-permute-start.3 = (bf16[32,64]{1,0:T(8,128)(2,1)S(1)}, bf16[32,64]{1,0:T(8,128)(2,1)S(1)}, u32[]{:S(2)}, u32[]{:S(2)}) collective-permute-start(bf16[32,64]{1,0:T(8,128)(2,1)S(1)} %get-tuple-element.22), channel_id=1, source_target_pairs={{1,0},{2,1},{3,2},{4,3},{5,4},{6,5},{7,6},{8,7},{9,8},{10,9},{11,1... | collective-permute-start | bytes 12296 | tf_op jit(solution)/shard_map/ppermute | solution.py:26
  385.9 91.9 %copy-start.12 = (s32[4,256]{1,0:T(4,128)S(1)}, s32[4,256]{1,0:T(4,128)}, u32[]{:S(2)}) copy-start(s32[4,256]{1,0:T(4,128)} %copy-done.10) | copy-start | bytes 12292
  385.9 91.9 %copy-start.15 = (s32[4,256]{1,0:T(4,128)S(1)}, s32[4,256]{1,0:T(4,128)}, u32[]{:S(2)}) copy-start(s32[4,256]{1,0:T(4,128)} %copy-done.13) | copy-start | bytes 12292
  385.9 91.9 %copy-start.19 = (s32[4,128]{1,0:T(4,128)S(1)}, s32[4,128]{1,0:T(4,128)}, u32[]{:S(2)}) copy-start(s32[4,128]{1,0:T(4,128)} %copy-done.17) | copy-start | bytes 6148
  385.9 91.9 %copy-start.24 = (s32[512]{0:T(512)S(1)}, s32[512]{0:T(512)}, u32[]{:S(2)}) copy-start(s32[512]{0:T(512)} %copy-done.22) | copy-start | bytes 6148
  385.9 91.9 %copy-start.28 = (pred[4,256]{1,0:T(4,128)(4,1)S(1)}, pred[4,256]{1,0:T(4,128)(4,1)}, u32[]{:S(2)}) copy-start(pred[4,256]{1,0:T(4,128)(4,1)} %copy-done.26) | copy-start | bytes 3076
  389.9 60.5 %copy-start = (f32[32,4,128]{0,2,1:T(8,128)}, f32[32,4,128]{0,2,1:T(8,128)S(1)}, u32[]{:S(2)}) copy-start(f32[32,4,128]{0,2,1:T(8,128)S(1)} %copy.96) | copy-start | bytes 196612
  419.4 31.0 %copy-start.9 = (f32[32]{0:T(128)}, f32[32]{0:T(128)S(1)}, u32[]{:S(2)}) copy-start(f32[32]{0:T(128)S(1)} %div.65) | copy-start | bytes 388
  447.1 36.0 %copy-start.29 = (f32[32]{0:T(128)}, f32[32]{0:T(128)S(1)}, u32[]{:S(2)}) copy-start(f32[32]{0:T(128)S(1)} %reduce_sum.137) | copy-start | bytes 388
  447.7 2.7 copy-start.16
  450.4 32.7 %all-to-all-start.8 = ((bf16[32,32,512]{2,1,0:T(8,128)(2,1)}), bf16[32,32,512]{2,1,0:T(8,128)(2,1)S(1)}, u32[]{:S(2)}, u32[]{:S(2)}) async-start(bf16[32,32,512]{2,1,0:T(8,128)(2,1)} %broadcast_in_dim.45), calls=%async_computation.8 | async-start | bytes 2097152 | tf_op jit(solution)/shard_map/all_to_all | solution.py:43
  456.3 21.3 %collective-permute-start.4 = (bf16[32,64]{1,0:T(8,128)(2,1)S(1)}, bf16[32,64]{1,0:T(8,128)(2,1)S(1)}, u32[]{:S(2)}, u32[]{:S(2)}) collective-permute-start(bf16[32,64]{1,0:T(8,128)(2,1)S(1)} %get-tuple-element.15), channel_id=1, source_target_pairs={{0,1},{1,2},{2,3},{3,4},{4,5},{5,6},{6,7},{7,8},{8,9},{9,10},{10,1... | collective-permute-start | bytes 12296 | tf_op jit(solution)/shard_map/ppermute | solution.py:24
  458.2 19.4 %collective-permute-start.5 = (bf16[32,64]{1,0:T(8,128)(2,1)S(1)}, bf16[32,64]{1,0:T(8,128)(2,1)S(1)}, u32[]{:S(2)}, u32[]{:S(2)}) collective-permute-start(bf16[32,64]{1,0:T(8,128)(2,1)S(1)} %get-tuple-element.16), channel_id=1, source_target_pairs={{1,0},{2,1},{3,2},{4,3},{5,4},{6,5},{7,6},{8,7},{9,8},{10,9},{11,1... | collective-permute-start | bytes 12296 | tf_op jit(solution)/shard_map/ppermute | solution.py:26
  484.3 4.7 copy-start.1
  485.0 33.0 %copy-start.30 = (f32[32]{0:T(128)S(1)}, f32[32]{0:T(128)}, u32[]{:S(2)}) copy-start(f32[32]{0:T(128)} %copy-done.29) | copy-start | bytes 388
